TPU v7x, 128 devices: a whole 4x4x4 slice. The times are simulated.
128 devices in a mesh: leaf: 16 (over z, x), panel: 8 (over y, core).
Axes of the slice: x: 4, y: 4, z: 4, core: 2. Of those that a mesh axis runs over, the one named last changes fastest.
Arguments:
- child_front: float32 [16, 2048, 2048], P('leaf', 'panel'), as said below
- child_panel: bfloat16 [16, 2048, 4096], P('leaf'), may hold values from -0.03125 to 0.03125
- parent_front: float32 [4096, 4096], P('leaf', 'panel'), as said below
- tile_map: int32 [16, 8], P('leaf'), may hold values from 0 to 15, as said below
- tile_count: int32 [16], P('leaf'), may hold values from 2 to 8, as said below
Outputs:
- eliminated: float32 [4096, 4096], P('leaf', 'panel')
Inputs may be any that keep to these rules, and one draw needn't show every extreme that they name: `tile_count`: some child has 8 live tiles and some child has 2. `tile_map`: for child c the first tile_count[c] entries are distinct and rising; the other entries are 0. Each child's block is symmetric, and child_front[c] - child_panel[c] child_panel[c]^T is positive definite. `parent_front`: symmetric positive definite.
All inputs are finite; a program needn't handle non-finite values.
Results may differ from a plain program's by a relative error of at most 0.0003.
Values sent between devices are 32-bit elements; how exact they have to be, the bound alone decides.
No kernel may reach another device: no remote copies, remote signals or barrier semaphores. Data moves between devices by JAX's collectives and lax.ppermute only.
A program may use at most 128 MiB of HBM per device.

v0:
```python
import jax
import jax.numpy as jnp
from jax import lax
from jax.sharding import PartitionSpec as P

TILE = 256
NF = 4096
CB = 2048
STEPS = 4


def spread(array, axis, root):
    mine = lax.axis_index(axis) == root
    return lax.psum(jnp.where(mine, array, jnp.zeros_like(array)), axis)


def finish_rows(block, row_index, factor, pivot_start):
    solved = lax.linalg.triangular_solve(
        factor, block, left_side=False, lower=True, transpose_a=True
    )
    offset = jnp.clip(row_index - pivot_start, 0, TILE - 1)
    own_rows = jnp.take(factor, offset, axis=0)
    inside = (row_index >= pivot_start) & (row_index < pivot_start + TILE)
    kept = jnp.where(inside[:, None], own_rows, solved)
    return jnp.where(row_index[:, None] < pivot_start, 0.0, kept)


def shards(child_front, child_panel, parent_front, tile_map, tile_count):
    highest = lax.Precision.HIGHEST
    panel_count = lax.axis_size("panel")
    leaf_id = lax.axis_index("leaf")
    panel_id = lax.axis_index("panel")
    tiles_child = CB // TILE
    tiles_front = NF // TILE
    pivot_span = STEPS * TILE
    child_rows = child_front.shape[1]
    height = parent_front.shape[0]
    col_width = parent_front.shape[1]
    panel_all = child_panel[0]
    own_panel = lax.dynamic_slice_in_dim(panel_all, panel_id * child_rows, child_rows, 0)
    update = child_front[0] - lax.dot_general(
        own_panel, panel_all, (((1,), (1,)), ((), ())), preferred_element_type=jnp.float32
    )
    mapped = tile_map[0]
    live_tiles = jnp.arange(tiles_child, dtype=jnp.int32) < tile_count[0]
    everywhere = jnp.arange(tiles_front, dtype=jnp.int32)
    chosen = ((mapped[None, :] == everywhere[:, None]) & live_tiles[None, :]).astype(jnp.float32)
    placed = jnp.einsum(
        "rtb,ft->rfb", update.reshape(child_rows, tiles_child, TILE), chosen, precision=highest
    )
    placed = placed.reshape(child_rows, panel_count, col_width)
    moved_cols = lax.all_to_all(placed, "panel", split_axis=1, concat_axis=0, tiled=True)
    column_tiles = moved_cols.reshape(tiles_child, TILE, col_width)
    targets = jnp.arange(lax.axis_size("leaf") * height // TILE, dtype=jnp.int32)
    picked = ((mapped[None, :] == targets[:, None]) & live_tiles[None, :]).astype(jnp.float32)
    front_block = parent_front + lax.psum_scatter(
        jnp.einsum("ft,tbc->fbc", picked, column_tiles, precision=highest).reshape(
            lax.axis_size("leaf") * height, col_width
        ),
        "leaf",
        scatter_dimension=0,
        tiled=True,
    )
    global_rows = leaf_id * height + jnp.arange(height, dtype=jnp.int32)
    global_cols = panel_id * col_width + jnp.arange(col_width, dtype=jnp.int32)
    col_tiles = col_width // TILE
    for pivot_step in range(STEPS):
        source_panel = pivot_step // col_tiles
        local_start = pivot_step % col_tiles * TILE
        pivot_start = pivot_step * TILE
        source = front_block[:, local_start : local_start + TILE]
        column = spread(source, "panel", source_panel)
        full_column = lax.all_gather(column, "leaf", axis=0, tiled=True)
        factor = jnp.linalg.cholesky(full_column[pivot_start : pivot_start + TILE])
        own_factor = finish_rows(column, global_rows, factor, pivot_start)
        col_factor = finish_rows(
            lax.dynamic_slice_in_dim(full_column, panel_id * col_width, col_width, 0),
            global_cols,
            factor,
            pivot_start,
        )
        front_block = front_block - lax.dot_general(
            own_factor,
            col_factor,
            (((1,), (1,)), ((), ())),
            precision=highest,
            preferred_element_type=jnp.float32,
        )
        replaced = jnp.where(
            panel_id == source_panel, own_factor, front_block[:, local_start : local_start + TILE]
        )
        front_block = front_block.at[:, local_start : local_start + TILE].set(replaced)
    upper_zone = (global_rows[:, None] < pivot_span) & (global_cols[None, :] >= pivot_span)
    return jnp.where(upper_zone, 0.0, front_block)


def solution(mesh):
    placed = (
        P("leaf", "panel", None),
        P("leaf", None, None),
        P("leaf", "panel"),
        P("leaf", None),
        P("leaf"),
    )
    return jax.shard_map(
        shards, mesh=mesh, in_specs=placed, out_specs=P("leaf", "panel"), check_vma=False
    )
```

profile of v0, /device:TPU:0, one launch (start us, length us, event | category | flops | bytes accessed | tf_op | source)
XLA Modules:
  0.0 964.4 jit_solution(7068307118465232745)
XLA Ops:
  6.5 11.5 %fusion.2 = f32[256,2048]{1,0:T(8,128)S(1)} fusion(bf16[1,2048,4096]{2,1,0:T(8,128)(2,1)} %param.23, f32[1,256,2048]{2,1,0:T(8,128)} %param.22, s32[]{:T(128)S(6)} %select_n.120), kind=kOutput, calls=%fused_computation.18 | convolution fusion | flops 4295491584 | bytes 23068676 | tf_op jit(solution)/shard_map/dot_general | solution.py:41
  23.2 5.2 reshape.226
  33.0 54.3 %all_to_all.15 = f32[256,8,512]{2,0,1:T(8,128)} all-to-all(f32[256,8,512]{2,0,1:T(8,128)S(1)} %copy.25), channel_id=1, replica_groups=mesh['leaf'=16,'panel'=8] {'panel'}, dimensions={1} | all-to-all | bytes 8388608 | tf_op jit(solution)/shard_map/all_to_all | solution.py:52
  87.4 5.5 copy.46
  92.8 5.5 fusion.118
  98.4 11.3 %copy.54 = f32[64,8,16,256]{3,1,2,0:T(8,128)} copy(f32[64,8,16,256]{3,2,1,0:T(8,128)S(1)} %bitcast.200) | data formatting | bytes 16777216
  110.9 85.6 %reduce-scatter.2.cloned.1.call-done = f32[256,512]{0,1:T(8,128)} async-done(((f32[4096,512]{0,1:T(8,128)}), f32[256,512]{0,1:T(8,128)}) %reduce-scatter.2.cloned.1.call-update) | async-done | bytes 524304 | tf_op jit(solution)/shard_map/reduce_scatter | solution.py:56
  198.4 60.0 %all-reduce.6.cloned.1.call-done = f32[256,256]{0,1:T(8,128)} async-done(((f32[256,256]{0,1:T(8,128)}), f32[256,256]{0,1:T(8,128)}) %all-reduce.6.cloned.1.call-update) | async-done | bytes 262160 | tf_op jit(solution)/shard_map/psum | solution.py:14
  259.5 57.1 %all-gather.5.cloned.1.call-done = f32[4096,256]{0,1:T(8,128)} async-done(((f32[256,256]{0,1:T(8,128)}), f32[4096,256]{0,1:T(8,128)}) %all-gather.5.cloned.1.call-update) | async-done | bytes 4194320 | tf_op jit(solution)/shard_map/all_gather | solution.py:73
  318.7 11.7 %cholesky.214 = f32[128,128]{1,0:T(8,128)S(1)} custom-call(f32[128,128]{1,0:T(8,128)S(1)} %cholesky.346), custom_call_target="Cholesky" | custom-call | tf_op jit(solution)/shard_map/jit(cholesky)/cholesky | solution.py:74
  330.4 9.8 %custom-call.23 = f32[1,128,128]{1,2,0:T(8,128)S(1)} custom-call(f32[1,128,128]{2,1,0:T(8,128)S(1)} %get-tuple-element.181), custom_call_target="InvertDiagBlocksLowerTriangular" | custom-call | tf_op jit(solution)/shard_map/jit(cholesky)/cholesky | solution.py:74
  340.7 11.7 %cholesky.231 = f32[128,128]{1,0:T(8,128)S(1)} custom-call(f32[128,128]{1,0:T(8,128)S(1)} %convolution_subtract_fusion.15), custom_call_target="Cholesky" | custom-call | tf_op jit(solution)/shard_map/jit(cholesky)/cholesky | solution.py:74
  358.8 20.1 %custom-call.24 = f32[2,128,128]{1,2,0:T(8,128)S(1)} custom-call(f32[2,128,128]{2,1,0:T(8,128)S(1)} %get-tuple-element.110), custom_call_target="InvertDiagBlocksLowerTriangular" | custom-call | tf_op jit(solution)/shard_map/triangular_solve/custom-call.0 | solution.py:18
  388.4 59.7 %all-reduce.8.cloned.1.call-done = f32[256,256]{0,1:T(8,128)} async-done(((f32[256,256]{0,1:T(8,128)}), f32[256,256]{0,1:T(8,128)}) %all-reduce.8.cloned.1.call-update) | async-done | bytes 262160 | tf_op jit(solution)/shard_map/psum | solution.py:14
  448.5 57.6 %all-gather.7.cloned.1.call-done = f32[4096,256]{0,1:T(8,128)} async-done(((f32[256,256]{0,1:T(8,128)}), f32[4096,256]{0,1:T(8,128)}) %all-gather.7.cloned.1.call-update) | async-done | bytes 4194320 | tf_op jit(solution)/shard_map/all_gather | solution.py:73
  508.3 11.7 %cholesky.248 = f32[128,128]{1,0:T(8,128)S(1)} custom-call(f32[128,128]{1,0:T(8,128)S(1)} %cholesky.349), custom_call_target="Cholesky" | custom-call | tf_op jit(solution)/shard_map/jit(cholesky)/cholesky | solution.py:74
  520.1 9.8 %custom-call.26 = f32[1,128,128]{1,2,0:T(8,128)S(1)} custom-call(f32[1,128,128]{2,1,0:T(8,128)S(1)} %get-tuple-element.177), custom_call_target="InvertDiagBlocksLowerTriangular" | custom-call | tf_op jit(solution)/shard_map/jit(cholesky)/cholesky | solution.py:74
  530.3 11.7 %cholesky.265 = f32[128,128]{1,0:T(8,128)S(1)} custom-call(f32[128,128]{1,0:T(8,128)S(1)} %convolution_subtract_fusion.14), custom_call_target="Cholesky" | custom-call | tf_op jit(solution)/shard_map/jit(cholesky)/cholesky | solution.py:74
  549.3 19.7 %custom-call.27 = f32[2,128,128]{1,2,0:T(8,128)S(1)} custom-call(f32[2,128,128]{2,1,0:T(8,128)S(1)} %get-tuple-element.112), custom_call_target="InvertDiagBlocksLowerTriangular" | custom-call | tf_op jit(solution)/shard_map/triangular_solve/custom-call.0 | solution.py:18
  577.8 59.7 %all-reduce.10.cloned.1.call-done = f32[256,256]{0,1:T(8,128)} async-done(((f32[256,256]{0,1:T(8,128)}), f32[256,256]{0,1:T(8,128)}) %all-reduce.10.cloned.1.call-update) | async-done | bytes 262160 | tf_op jit(solution)/shard_map/psum | solution.py:14
  637.9 57.7 %all-gather.9.cloned.1.call-done = f32[4096,256]{0,1:T(8,128)} async-done(((f32[256,256]{0,1:T(8,128)}), f32[4096,256]{0,1:T(8,128)}) %all-gather.9.cloned.1.call-update) | async-done | bytes 4194320 | tf_op jit(solution)/shard_map/all_gather | solution.py:73
  697.7 11.7 %cholesky.282 = f32[128,128]{1,0:T(8,128)S(1)} custom-call(f32[128,128]{1,0:T(8,128)S(1)} %cholesky.352), custom_call_target="Cholesky" | custom-call | tf_op jit(solution)/shard_map/jit(cholesky)/cholesky | solution.py:74
  709.5 9.8 %custom-call.29 = f32[1,128,128]{1,2,0:T(8,128)S(1)} custom-call(f32[1,128,128]{2,1,0:T(8,128)S(1)} %get-tuple-element.173), custom_call_target="InvertDiagBlocksLowerTriangular" | custom-call | tf_op jit(solution)/shard_map/jit(cholesky)/cholesky | solution.py:74
  719.8 11.7 %cholesky.299 = f32[128,128]{1,0:T(8,128)S(1)} custom-call(f32[128,128]{1,0:T(8,128)S(1)} %convolution_subtract_fusion.13), custom_call_target="Cholesky" | custom-call | tf_op jit(solution)/shard_map/jit(cholesky)/cholesky | solution.py:74
  734.3 4.6 while.22
  739.0 19.7 %custom-call.30 = f32[2,128,128]{1,2,0:T(8,128)S(1)} custom-call(f32[2,128,128]{2,1,0:T(8,128)S(1)} %get-tuple-element.114), custom_call_target="InvertDiagBlocksLowerTriangular" | custom-call | tf_op jit(solution)/shard_map/triangular_solve/custom-call.0 | solution.py:18
  768.4 59.5 %all-reduce.12.cloned.1.call-done = f32[256,256]{0,1:T(8,128)} async-done(((f32[256,256]{0,1:T(8,128)}), f32[256,256]{0,1:T(8,128)}) %all-reduce.12.cloned.1.call-update) | async-done | bytes 262160 | tf_op jit(solution)/shard_map/psum | solution.py:14
  828.0 58.0 %all-gather.11.cloned.1.call-done = f32[4096,256]{0,1:T(8,128)} async-done(((f32[256,256]{0,1:T(8,128)}), f32[4096,256]{0,1:T(8,128)}) %all-gather.11.cloned.1.call-update) | async-done | bytes 4194320 | tf_op jit(solution)/shard_map/all_gather | solution.py:73
  888.1 11.7 %cholesky.316 = f32[128,128]{1,0:T(8,128)S(1)} custom-call(f32[128,128]{1,0:T(8,128)S(1)} %cholesky.355), custom_call_target="Cholesky" | custom-call | tf_op jit(solution)/shard_map/jit(cholesky)/cholesky | solution.py:74
  899.9 9.8 %custom-call.32 = f32[1,128,128]{1,2,0:T(8,128)S(1)} custom-call(f32[1,128,128]{2,1,0:T(8,128)S(1)} %get-tuple-element.169), custom_call_target="InvertDiagBlocksLowerTriangular" | custom-call | tf_op jit(solution)/shard_map/jit(cholesky)/cholesky | solution.py:74
  910.2 11.7 %cholesky.333 = f32[128,128]{1,0:T(8,128)S(1)} custom-call(f32[128,128]{1,0:T(8,128)S(1)} %convolution_subtract_fusion.12), custom_call_target="Cholesky" | custom-call | tf_op jit(solution)/shard_map/jit(cholesky)/cholesky | solution.py:74
  928.8 19.7 %custom-call.33 = f32[2,128,128]{1,2,0:T(8,128)S(1)} custom-call(f32[2,128,128]{2,1,0:T(8,128)S(1)} %get-tuple-element.116), custom_call_target="InvertDiagBlocksLowerTriangular" | custom-call | tf_op jit(solution)/shard_map/triangular_solve/custom-call.0 | solution.py:18
  (202 shorter events, 95.5 us)
Async XLA Ops:
  6.5 190.0 %reduce-scatter.2.cloned.1.call-start = ((), (), s32[]{:S(2)}) async-start(), calls=%async_computation.2 | async-start | bytes 8912896 | tf_op jit(solution)/shard_map/reduce_scatter | solution.py:56
  18.0 1.6 copy-start.5
  109.7 1.0 copy-start.4
  109.7 148.7 %all-reduce.6.cloned.1.call-start = ((), (), s32[]{:S(2)}) async-start(), calls=%async_computation.3 | async-start | bytes 524288 | tf_op jit(solution)/shard_map/psum | solution.py:14
  198.3 118.2 %all-gather.5.cloned.1.call-start = ((), (), s32[]{:S(2)}) async-start(), calls=%async_computation.4 | async-start | bytes 4456448 | tf_op jit(solution)/shard_map/all_gather | solution.py:73
  258.4 120.5 %copy-start = (f32[256,256]{0,1:T(8,128)S(1)}, f32[256,256]{0,1:T(8,128)}, u32[]{:S(2)}) copy-start(f32[256,256]{0,1:T(8,128)} %all-reduce.6.cloned.1.call-done) | copy-start | bytes 786436
  258.4 189.7 %all-reduce.8.cloned.1.call-start = ((), (), s32[]{:S(2)}) async-start(), calls=%async_computation.5 | async-start | bytes 524288 | tf_op jit(solution)/shard_map/psum | solution.py:14
  388.4 117.8 %all-gather.7.cloned.1.call-start = ((), (), s32[]{:S(2)}) async-start(), calls=%async_computation.6 | async-start | bytes 4456448 | tf_op jit(solution)/shard_map/all_gather | solution.py:73
  448.2 120.8 %copy-start.2 = (f32[256,256]{0,1:T(8,128)S(1)}, f32[256,256]{0,1:T(8,128)}, u32[]{:S(2)}) copy-start(f32[256,256]{0,1:T(8,128)} %all-reduce.8.cloned.1.call-done) | copy-start | bytes 786436
  448.2 189.3 %all-reduce.10.cloned.1.call-start = ((), (), s32[]{:S(2)}) async-start(), calls=%async_computation.7 | async-start | bytes 524288 | tf_op jit(solution)/shard_map/psum | solution.py:14
  577.8 117.9 %all-gather.9.cloned.1.call-start = ((), (), s32[]{:S(2)}) async-start(), calls=%async_computation.8 | async-start | bytes 4456448 | tf_op jit(solution)/shard_map/all_gather | solution.py:73
  637.5 121.2 %copy-start.3 = (f32[256,256]{0,1:T(8,128)S(1)}, f32[256,256]{0,1:T(8,128)}, u32[]{:S(2)}) copy-start(f32[256,256]{0,1:T(8,128)} %all-reduce.10.cloned.1.call-done) | copy-start | bytes 786436
  637.5 190.3 %all-reduce.12.cloned.1.call-start = ((), (), s32[]{:S(2)}) async-start(), calls=%async_computation.9 | async-start | bytes 524288 | tf_op jit(solution)/shard_map/psum | solution.py:14
  768.1 117.9 %all-gather.11.cloned.1.call-start = ((), (), s32[]{:S(2)}) async-start(), calls=%async_computation.10 | async-start | bytes 4456448 | tf_op jit(solution)/shard_map/all_gather | solution.py:73
  827.8 120.6 %copy-start.1 = (f32[256,256]{0,1:T(8,128)S(1)}, f32[256,256]{0,1:T(8,128)}, u32[]{:S(2)}) copy-start(f32[256,256]{0,1:T(8,128)} %all-reduce.12.cloned.1.call-done) | copy-start | bytes 786436
Sparse Core Ops, SparseCore 0:
  109.8 86.6 reduce-scatter.1
  198.8 59.5 all-reduce.5
  260.5 55.9 all-gather.4
  388.5 59.6 all-reduce.7
  450.1 55.9 all-gather.6
  577.9 59.5 all-reduce.9
  639.6 55.9 all-gather.8
  768.3 59.5 all-reduce.11
  830.0 55.9 all-gather.10
where the time goes:
time: 972 us; the launch traced here: 964 us
  waiting for transfers between devices  555 us (57%)
  other arithmetic  228 us (23%)
  local copies, waits for them, and re-layouts  62 us (6%)
  blocking collectives  54.3 us (6%)
  matrix products  42.7 us (4%)
  between operations  20.3 us (2%)
    psum x4, waiting for transfers between devices, spread(): return lax.psum(jnp.where(mine, array, jnp.zeros_like(array)), axis)  239 us
    all_gather x4, waiting for transfers between devices, shards(): full_column = lax.all_gather(column, 'leaf', axis=0, tiled=True)  230 us
    another operation x27, other arithmetic, shards(): factor = jnp.linalg.cholesky(full_column[pivot_start:pivot_start + TILE])  138 us
    reduce_scatter x1, waiting for transfers between devices, shards(): lax.psum_scatter(jnp.einsum('ft,tbc->fbc', picked, column_tiles, precisio...  85.6 us
    another operation x9, other arithmetic, finish_rows(): lax.linalg.triangular_solve(factor, block, left_side=False, lower=True, t...  79.3 us
    all_to_all x1, blocking collectives, shards(): lax.all_to_all(placed, 'panel', split_axis=1, concat_axis=0, tiled=True)  54.3 us
  transfers between devices with their start and end apart: 9, of which 9 were waited for; matrix products, arithmetic and copies ran while one was open for 0% of the time, Pallas kernels for 0%

commit v1 on v0

--- a/solution.py
+++ b/solution.py
@@ -7,6 +7,22 @@
 NF = 4096
 CB = 2048
 STEPS = 4
+
+
+def pairwise_exchange(x, axis, split, join):
+    ways, here = (lax.axis_size(axis), lax.axis_index(axis))
+    width = x.shape[split] // ways
+    lengths = list(x.shape)
+    lengths[split] = width
+    height = lengths[join]
+    lengths[join] = height * ways
+    full = jnp.zeros(lengths, x.dtype)
+    for mask in range(ways):
+        part = lax.dynamic_slice_in_dim(x, (here ^ mask) * width, width, axis=split)
+        if mask:
+            part = lax.ppermute(part, axis, [(d, d ^ mask) for d in range(ways)])
+        full = lax.dynamic_update_slice_in_dim(full, part, (here ^ mask) * height, axis=join)
+    return full
 
 
 def spread(array, axis, root):
@@ -49,7 +65,7 @@
         "rtb,ft->rfb", update.reshape(child_rows, tiles_child, TILE), chosen, precision=highest
     )
     placed = placed.reshape(child_rows, panel_count, col_width)
-    moved_cols = lax.all_to_all(placed, "panel", split_axis=1, concat_axis=0, tiled=True)
+    moved_cols = pairwise_exchange(placed, "panel", 1, 0)
     column_tiles = moved_cols.reshape(tiles_child, TILE, col_width)
     targets = jnp.arange(lax.axis_size("leaf") * height // TILE, dtype=jnp.int32)
     picked = ((mapped[None, :] == targets[:, None]) & live_tiles[None, :]).astype(jnp.float32)

time: 972 us -> 993 us (1.022)
  blocking collectives: 54.3 us -> 0 us
  local copies, waits for them, and re-layouts: 62 us -> 89.7 us
  waiting for transfers between devices: 555 us -> 578 us
  starting transfers between devices: 1.13 us -> 23.5 us
    all_to_all x1 -> x0, blocking collectives: 54.3 us -> none  [shards(): lax.all_to_all(placed, 'panel', split_axis=1, concat_axis=0, tiled=True)]
    ppermute x0 -> x7, waiting for transfers between devices: none -> 33.6 us  [pairwise_exchange(): part = lax.ppermute(part, axis, [(d, d ^ mask) for d in range(ways)])]
    dynamic_slice x0 -> x1, local copies, waits for them, and re-layouts: none -> 16.4 us  [pairwise_exchange(): part = lax.dynamic_slice_in_dim(x, (here ^ mask) * width, width, axis=split)]
    dynamic_update_slice x0 -> x8, local copies, waits for them, and re-layouts: none -> 11.9 us  [pairwise_exchange(): lax.dynamic_update_slice_in_dim(full, part, (here ^ mask) * height, axis=...]
    all_gather x4, waiting for transfers between devices: 230 us -> 219 us  [shards(): full_column = lax.all_gather(column, 'leaf', axis=0, tiled=True)]
    psum x4, starting transfers between devices: 0.79 us -> 12.4 us  [spread(): return lax.psum(jnp.where(mine, array, jnp.zeros_like(array)), axis)]
    ppermute x0 -> x7, starting transfers between devices: none -> 10.7 us  [pairwise_exchange(): part = lax.ppermute(part, axis, [(d, d ^ mask) for d in range(ways)])]
  transfers between devices with their start and end apart: 9 -> 16, of which waited for: 9 -> 14; matrix products, arithmetic and copies ran while one was open for 0% -> 2% of each run, Pallas kernels for 0% -> 0%
where the time goes in v1:
time: 993 us; the launch traced here: 984 us
  waiting for transfers between devices  578 us (58%)
  other arithmetic  227 us (23%)
  local copies, waits for them, and re-layouts  89.7 us (9%)
  matrix products  42.7 us (4%)
  starting transfers between devices  23.5 us (2%)
  between operations  20.7 us (2%)
    psum x4, waiting for transfers between devices, spread(): return lax.psum(jnp.where(mine, array, jnp.zeros_like(array)), axis)  239 us
    all_gather x4, waiting for transfers between devices, shards(): full_column = lax.all_gather(column, 'leaf', axis=0, tiled=True)  219 us
    another operation x27, other arithmetic, shards(): factor = jnp.linalg.cholesky(full_column[pivot_start:pivot_start + TILE])  138 us
    reduce_scatter x1, waiting for transfers between devices, shards(): lax.psum_scatter(jnp.einsum('ft,tbc->fbc', picked, column_tiles, precisio...  86.8 us
    another operation x9, other arithmetic, finish_rows(): lax.linalg.triangular_solve(factor, block, left_side=False, lower=True, t...  78.8 us
    ppermute x7, waiting for transfers between devices, pairwise_exchange(): part = lax.ppermute(part, axis, [(d, d ^ mask) for d in range(ways)])  33.6 us
  transfers between devices with their start and end apart: 16, of which 14 were waited for; matrix products, arithmetic and copies ran while one was open for 2% of the time, Pallas kernels for 0%

profile of v1, /device:TPU:0, one launch (start us, length us, event | category | flops | bytes accessed | tf_op | source)
XLA Modules:
  0.0 983.6 jit_solution(4830645480521095008)
XLA Ops:
  6.5 11.5 %fusion.2 = f32[256,2048]{1,0:T(8,128)S(1)} fusion(bf16[1,2048,4096]{2,1,0:T(8,128)(2,1)} %param.23, f32[1,256,2048]{2,1,0:T(8,128)} %param.22, s32[]{:T(128)S(6)} %select_n.166), kind=kOutput, calls=%fused_computation.18 | convolution fusion | flops 4295491584 | bytes 23068676 | tf_op jit(solution)/shard_map/dot_general | solution.py:57
  28.4 16.4 %constant_dynamic-slice_fusion.4 = (f32[256,1,512]{2,1,0:T(1,128)S(1)}, f32[256,1,512]{2,1,0:T(1,128)S(1)}, f32[256,1,512]{2,1,0:T(1,128)S(1)}, f32[256,1,512]{2...) fusion(f32[256,8,512]{2,1,0:T(8,128)} %reshape.225, ...), kind=kLoop, calls=%fused_computation.192 | loop fusion | bytes 8388640 | tf_op jit(solution)/shard_map/dynamic_slice | solution.py:21
  64.7 6.3 collective-permute-done.2
  72.8 12.9 %collective-permute-done.3 = f32[256,1,512]{2,0,1:T(8,128)} collective-permute-done((f32[256,1,512]{2,0,1:T(8,128)S(1)}, f32[256,1,512]{2,0,1:T(8,128)}, u32[]{:S(2)}, u32[]{:S(2)}) %collective-permute-start.3) | collective-permute-done | bytes 524320 | tf_op jit(solution)/shard_map/ppermute | solution.py:23
  87.6 8.4 collective-permute-done.4
  116.5 11.3 %copy.69 = f32[64,8,16,256]{3,1,2,0:T(8,128)} copy(f32[64,8,16,256]{3,2,1,0:T(8,128)S(1)} %bitcast.197) | data formatting | bytes 16777216
  129.0 86.8 %reduce-scatter.2.cloned.1.call-done = f32[256,512]{0,1:T(8,128)} async-done(((f32[4096,512]{0,1:T(8,128)}), f32[256,512]{0,1:T(8,128)}) %reduce-scatter.2.cloned.1.call-update) | async-done | bytes 524304 | tf_op jit(solution)/shard_map/reduce_scatter | solution.py:72
  217.7 60.1 %all-reduce.6.cloned.1.call-done = f32[256,256]{0,1:T(8,128)} async-done(((f32[256,256]{0,1:T(8,128)}), f32[256,256]{0,1:T(8,128)}) %all-reduce.6.cloned.1.call-update) | async-done | bytes 262160 | tf_op jit(solution)/shard_map/psum | solution.py:30
  277.8 11.9 %all-reduce.8.cloned.1.call-start = ((), (), s32[]{:S(2)}) async-start(), calls=%async_computation.4 | async-start | bytes 524288 | tf_op jit(solution)/shard_map/psum | solution.py:30
  290.5 45.4 %all-gather.5.cloned.1.call-done = f32[4096,256]{0,1:T(8,128)} async-done(((f32[256,256]{0,1:T(8,128)}), f32[4096,256]{0,1:T(8,128)}) %all-gather.5.cloned.1.call-update) | async-done | bytes 4194320 | tf_op jit(solution)/shard_map/all_gather | solution.py:89
  338.1 11.7 %cholesky.214 = f32[128,128]{1,0:T(8,128)S(1)} custom-call(f32[128,128]{1,0:T(8,128)S(1)} %cholesky.346), custom_call_target="Cholesky" | custom-call | tf_op jit(solution)/shard_map/jit(cholesky)/cholesky | solution.py:90
  349.8 9.8 custom-call.23
  360.1 11.7 %cholesky.231 = f32[128,128]{1,0:T(8,128)S(1)} custom-call(f32[128,128]{1,0:T(8,128)S(1)} %convolution_subtract_fusion.15), custom_call_target="Cholesky" | custom-call | tf_op jit(solution)/shard_map/jit(cholesky)/cholesky | solution.py:90
  378.1 19.7 %custom-call.24 = f32[2,128,128]{1,2,0:T(8,128)S(1)} custom-call(f32[2,128,128]{2,1,0:T(8,128)S(1)} %get-tuple-element.110), custom_call_target="InvertDiagBlocksLowerTriangular" | custom-call | tf_op jit(solution)/shard_map/triangular_solve/custom-call.0 | solution.py:34
  407.3 59.7 %all-reduce.8.cloned.1.call-done = f32[256,256]{0,1:T(8,128)} async-done(((f32[256,256]{0,1:T(8,128)}), f32[256,256]{0,1:T(8,128)}) %all-reduce.8.cloned.1.call-update) | async-done | bytes 262160 | tf_op jit(solution)/shard_map/psum | solution.py:30
  467.5 57.6 %all-gather.7.cloned.1.call-done = f32[4096,256]{0,1:T(8,128)} async-done(((f32[256,256]{0,1:T(8,128)}), f32[4096,256]{0,1:T(8,128)}) %all-gather.7.cloned.1.call-update) | async-done | bytes 4194320 | tf_op jit(solution)/shard_map/all_gather | solution.py:89
  527.2 11.7 %cholesky.248 = f32[128,128]{1,0:T(8,128)S(1)} custom-call(f32[128,128]{1,0:T(8,128)S(1)} %cholesky.349), custom_call_target="Cholesky" | custom-call | tf_op jit(solution)/shard_map/jit(cholesky)/cholesky | solution.py:90
  538.9 9.8 custom-call.26
  549.2 11.7 %cholesky.265 = f32[128,128]{1,0:T(8,128)S(1)} custom-call(f32[128,128]{1,0:T(8,128)S(1)} %convolution_subtract_fusion.14), custom_call_target="Cholesky" | custom-call | tf_op jit(solution)/shard_map/jit(cholesky)/cholesky | solution.py:90
  568.2 19.7 %custom-call.27 = f32[2,128,128]{1,2,0:T(8,128)S(1)} custom-call(f32[2,128,128]{2,1,0:T(8,128)S(1)} %get-tuple-element.112), custom_call_target="InvertDiagBlocksLowerTriangular" | custom-call | tf_op jit(solution)/shard_map/triangular_solve/custom-call.0 | solution.py:34
  596.8 59.7 %all-reduce.10.cloned.1.call-done = f32[256,256]{0,1:T(8,128)} async-done(((f32[256,256]{0,1:T(8,128)}), f32[256,256]{0,1:T(8,128)}) %all-reduce.10.cloned.1.call-update) | async-done | bytes 262160 | tf_op jit(solution)/shard_map/psum | solution.py:30
  656.9 57.8 %all-gather.9.cloned.1.call-done = f32[4096,256]{0,1:T(8,128)} async-done(((f32[256,256]{0,1:T(8,128)}), f32[4096,256]{0,1:T(8,128)}) %all-gather.9.cloned.1.call-update) | async-done | bytes 4194320 | tf_op jit(solution)/shard_map/all_gather | solution.py:89
  716.8 11.7 %cholesky.282 = f32[128,128]{1,0:T(8,128)S(1)} custom-call(f32[128,128]{1,0:T(8,128)S(1)} %cholesky.352), custom_call_target="Cholesky" | custom-call | tf_op jit(solution)/shard_map/jit(cholesky)/cholesky | solution.py:90
  728.6 9.8 custom-call.29
  738.9 11.7 %cholesky.299 = f32[128,128]{1,0:T(8,128)S(1)} custom-call(f32[128,128]{1,0:T(8,128)S(1)} %convolution_subtract_fusion.13), custom_call_target="Cholesky" | custom-call | tf_op jit(solution)/shard_map/jit(cholesky)/cholesky | solution.py:90
  757.6 19.7 %custom-call.30 = f32[2,128,128]{1,2,0:T(8,128)S(1)} custom-call(f32[2,128,128]{2,1,0:T(8,128)S(1)} %get-tuple-element.114), custom_call_target="InvertDiagBlocksLowerTriangular" | custom-call | tf_op jit(solution)/shard_map/triangular_solve/custom-call.0 | solution.py:34
  787.1 59.5 %all-reduce.12.cloned.1.call-done = f32[256,256]{0,1:T(8,128)} async-done(((f32[256,256]{0,1:T(8,128)}), f32[256,256]{0,1:T(8,128)}) %all-reduce.12.cloned.1.call-update) | async-done | bytes 262160 | tf_op jit(solution)/shard_map/psum | solution.py:30
  846.7 58.0 %all-gather.11.cloned.1.call-done = f32[4096,256]{0,1:T(8,128)} async-done(((f32[256,256]{0,1:T(8,128)}), f32[4096,256]{0,1:T(8,128)}) %all-gather.11.cloned.1.call-update) | async-done | bytes 4194320 | tf_op jit(solution)/shard_map/all_gather | solution.py:89
  906.8 11.7 %cholesky.316 = f32[128,128]{1,0:T(8,128)S(1)} custom-call(f32[128,128]{1,0:T(8,128)S(1)} %cholesky.355), custom_call_target="Cholesky" | custom-call | tf_op jit(solution)/shard_map/jit(cholesky)/cholesky | solution.py:90
  918.6 9.8 custom-call.32
  928.9 11.7 %cholesky.333 = f32[128,128]{1,0:T(8,128)S(1)} custom-call(f32[128,128]{1,0:T(8,128)S(1)} %convolution_subtract_fusion.12), custom_call_target="Cholesky" | custom-call | tf_op jit(solution)/shard_map/jit(cholesky)/cholesky | solution.py:90
  947.6 19.7 %custom-call.33 = f32[2,128,128]{1,2,0:T(8,128)S(1)} custom-call(f32[2,128,128]{2,1,0:T(8,128)S(1)} %get-tuple-element.116), custom_call_target="InvertDiagBlocksLowerTriangular" | custom-call | tf_op jit(solution)/shard_map/triangular_solve/custom-call.0 | solution.py:34
  (231 shorter events, 144.0 us)
Async XLA Ops:
  6.5 209.3 %reduce-scatter.2.cloned.1.call-start = ((), (), s32[]{:S(2)}) async-start(), calls=%async_computation.1 | async-start | bytes 8912896 | tf_op jit(solution)/shard_map/reduce_scatter | solution.py:72
  18.0 1.6 copy-start.5
  45.6 9.9 %collective-permute-start = (f32[256,1,512]{2,0,1:T(8,128)}, f32[256,1,512]{2,0,1:T(8,128)}, u32[]{:S(2)}, u32[]{:S(2)}) collective-permute-start(f32[256,1,512]{2,0,1:T(8,128)} %copy.61), channel_id=1, source_target_pairs={{0,1},{1,0},{2,3},{3,2},{4,5},{5,4},{6,7},{7,6},{8,9},{9,8},{10,11... | collective-permute-start | bytes 1572872 | tf_op jit(solution)/shard_map/ppermute | solution.py:23
  45.7 15.0 %collective-permute-start.1 = (f32[256,1,512]{2,0,1:T(8,128)S(1)}, f32[256,1,512]{2,0,1:T(8,128)}, u32[]{:S(2)}, u32[]{:S(2)}) collective-permute-start(f32[256,1,512]{2,0,1:T(8,128)S(1)} %copy.62), channel_id=1, source_target_pairs={{0,2},{1,3},{2,0},{3,1},{4,6},{5,7},{6,4},{7,5},{8,10},{9,11},{10,... | collective-permute-start | bytes 1572872 | tf_op jit(solution)/shard_map/ppermute | solution.py:23
  47.5 23.5 %collective-permute-start.2 = (f32[256,1,512]{2,0,1:T(8,128)S(1)}, f32[256,1,512]{2,0,1:T(8,128)}, u32[]{:S(2)}, u32[]{:S(2)}) collective-permute-start(f32[256,1,512]{2,0,1:T(8,128)S(1)} %copy.63), channel_id=1, source_target_pairs={{0,3},{1,2},{2,1},{3,0},{4,7},{5,6},{6,5},{7,4},{8,11},{9,10},{10,... | collective-permute-start | bytes 1572872 | tf_op jit(solution)/shard_map/ppermute | solution.py:23
  47.7 38.0 %collective-permute-start.3 = (f32[256,1,512]{2,0,1:T(8,128)S(1)}, f32[256,1,512]{2,0,1:T(8,128)}, u32[]{:S(2)}, u32[]{:S(2)}) collective-permute-start(f32[256,1,512]{2,0,1:T(8,128)S(1)} %copy.64), channel_id=1, source_target_pairs={{0,4},{1,5},{2,6},{3,7},{4,0},{5,1},{6,2},{7,3},{8,12},{9,13},{10,... | collective-permute-start | bytes 1572872 | tf_op jit(solution)/shard_map/ppermute | solution.py:23
  51.2 44.9 %collective-permute-start.4 = (f32[256,1,512]{2,0,1:T(8,128)S(1)}, f32[256,1,512]{2,0,1:T(8,128)}, u32[]{:S(2)}, u32[]{:S(2)}) collective-permute-start(f32[256,1,512]{2,0,1:T(8,128)S(1)} %copy.65), channel_id=1, source_target_pairs={{0,5},{1,4},{2,7},{3,6},{4,1},{5,0},{6,3},{7,2},{8,13},{9,12},{10,... | collective-permute-start | bytes 1572872 | tf_op jit(solution)/shard_map/ppermute | solution.py:23
  55.5 42.4 %collective-permute-start.5 = (f32[256,1,512]{2,0,1:T(8,128)}, f32[256,1,512]{2,0,1:T(8,128)S(1)}, u32[]{:S(2)}, u32[]{:S(2)}) collective-permute-start(f32[256,1,512]{2,0,1:T(8,128)} %copy.66), channel_id=1, source_target_pairs={{0,6},{1,7},{2,4},{3,5},{4,2},{5,3},{6,0},{7,1},{8,14},{9,15},{10,... | collective-permute-start | bytes 1572872 | tf_op jit(solution)/shard_map/ppermute | solution.py:23
  60.6 44.0 %collective-permute-start.6 = (f32[256,1,512]{2,0,1:T(8,128)S(1)}, f32[256,1,512]{2,0,1:T(8,128)S(1)}, u32[]{:S(2)}, u32[]{:S(2)}) collective-permute-start(f32[256,1,512]{2,0,1:T(8,128)S(1)} %copy.67), channel_id=1, source_target_pairs={{0,7},{1,6},{2,5},{3,4},{4,3},{5,2},{6,1},{7,0},{8,15},{9,14},{10,... | collective-permute-start | bytes 1572872 | tf_op jit(solution)/shard_map/ppermute | solution.py:23
  127.8 1.0 copy-start.4
  127.8 150.0 %all-reduce.6.cloned.1.call-start = ((), (), s32[]{:S(2)}) async-start(), calls=%async_computation.2 | async-start | bytes 524288 | tf_op jit(solution)/shard_map/psum | solution.py:30
  217.7 118.3 %all-gather.5.cloned.1.call-start = ((), (), s32[]{:S(2)}) async-start(), calls=%async_computation.3 | async-start | bytes 4456448 | tf_op jit(solution)/shard_map/all_gather | solution.py:89
  277.8 120.0 %copy-start = (f32[256,256]{0,1:T(8,128)S(1)}, f32[256,256]{0,1:T(8,128)}, u32[]{:S(2)}) copy-start(f32[256,256]{0,1:T(8,128)} %all-reduce.6.cloned.1.call-done) | copy-start | bytes 786436
  277.8 189.2 %all-reduce.8.cloned.1.call-start = ((), (), s32[]{:S(2)}) async-start(), calls=%async_computation.4 | async-start | bytes 524288 | tf_op jit(solution)/shard_map/psum | solution.py:30
  407.3 117.8 %all-gather.7.cloned.1.call-start = ((), (), s32[]{:S(2)}) async-start(), calls=%async_computation.5 | async-start | bytes 4456448 | tf_op jit(solution)/shard_map/all_gather | solution.py:89
  467.1 120.8 %copy-start.2 = (f32[256,256]{0,1:T(8,128)S(1)}, f32[256,256]{0,1:T(8,128)}, u32[]{:S(2)}) copy-start(f32[256,256]{0,1:T(8,128)} %all-reduce.8.cloned.1.call-done) | copy-start | bytes 786436
  467.1 189.4 %all-reduce.10.cloned.1.call-start = ((), (), s32[]{:S(2)}) async-start(), calls=%async_computation.6 | async-start | bytes 524288 | tf_op jit(solution)/shard_map/psum | solution.py:30
  596.7 117.9 %all-gather.9.cloned.1.call-start = ((), (), s32[]{:S(2)}) async-start(), calls=%async_computation.7 | async-start | bytes 4456448 | tf_op jit(solution)/shard_map/all_gather | solution.py:89
  656.5 120.8 %copy-start.3 = (f32[256,256]{0,1:T(8,128)S(1)}, f32[256,256]{0,1:T(8,128)}, u32[]{:S(2)}) copy-start(f32[256,256]{0,1:T(8,128)} %all-reduce.10.cloned.1.call-done) | copy-start | bytes 786436
  656.6 190.0 %all-reduce.12.cloned.1.call-start = ((), (), s32[]{:S(2)}) async-start(), calls=%async_computation.8 | async-start | bytes 524288 | tf_op jit(solution)/shard_map/psum | solution.py:30
  786.8 117.9 %all-gather.11.cloned.1.call-start = ((), (), s32[]{:S(2)}) async-start(), calls=%async_computation.9 | async-start | bytes 4456448 | tf_op jit(solution)/shard_map/all_gather | solution.py:89
  846.6 120.7 %copy-start.1 = (f32[256,256]{0,1:T(8,128)S(1)}, f32[256,256]{0,1:T(8,128)}, u32[]{:S(2)}) copy-start(f32[256,256]{0,1:T(8,128)} %all-reduce.12.cloned.1.call-done) | copy-start | bytes 786436
Sparse Core Ops, SparseCore 0:
  127.9 87.8 reduce-scatter.1
  218.1 59.6 all-reduce.5
  279.9 55.9 all-gather.4
  407.4 59.6 all-reduce.7
  469.0 55.9 all-gather.6
  596.9 59.6 all-reduce.9
  658.6 55.9 all-gather.8
  786.9 59.6 all-reduce.11
  848.7 55.9 all-gather.10
